TPU v7x, 256 devices: a whole 4x4x8 slice. The times are simulated.
256 devices in a mesh: child: 64 (over x, z_hi, y), tensor: 4 (over z_lo, core).
Axes of the slice: x: 4, y: 4, z: 8 (z_hi: 4, z_lo: 2; z = z_hi * 2 + z_lo), core: 2. Of those that a mesh axis runs over, the one named last changes fastest.
Arguments:
- tokens: bfloat16 [32768, 5120], P('child'), may hold values from -28 to 28
- episode: int32 [64, 512], P('child'), may hold values from 0 to 3, never falling along the last dimension, each value on 1 to 256 neighbouring positions
- parent_index: int32 [64], replicated, may hold values from 0 to 1
- mutation_seed: int32 [64], P('child'), may hold values from 0 to 1073741823
- elite_project: bfloat16 [2, 5120, 4, 896], P(None, 'child', 'tensor'), may hold values from -0.078125 to 0.078125
- elite_output: bfloat16 [2, 5120, 4, 640], P(None, 'child', 'tensor'), may hold values from -0.23925781 to 0.23925781
- elite_bias: float32 [2, 4, 896], P(None, 'tensor'), may hold values from -1.2 to 1.2
Outputs:
- attended: bfloat16 [32768, 5120], P('child', 'tensor')
Inputs may be any that keep to these rules, and one draw needn't show every extreme that they name: Along each member's rows the episode numbers never fall; each of the 4 episodes has 1 to 256 rows, and some episode has exactly 256.
All inputs are finite; a program needn't handle non-finite values.
Results may differ from a plain program's by a relative error of at most 0.007.
The roundings to bfloat16 on the way count: a program that leaves them out, or rounds other values in their place, can miss the bound.
Values may be sent and summed in bfloat16 or wider, within the bound.
No kernel may reach another device: no remote copies, remote signals or barrier semaphores. Data moves between devices by JAX's collectives and lax.ppermute only.
A program may use at most 128 MiB of HBM per device.

v0:
```python
import math

import jax
import jax.numpy as jnp
from jax import lax
from jax.sharding import PartitionSpec as P

D = 5120
HEAD_DIM = 128
KV_HEADS = 4
GROUP = 5


MUTATION = 0.25
BIAS_MUTATION = 0.05
ROPE_BASE = 1000000.0
NOISE_SPREAD = 147.80054


def mix_hash(seed_value, counter):
    hashed = counter + seed_value * jnp.int32(-1640531535)
    hashed = hashed ^ lax.shift_right_logical(hashed, jnp.full_like(hashed, 16))
    hashed = hashed * jnp.int32(-2048144789)
    hashed = hashed ^ lax.shift_right_logical(hashed, jnp.full_like(hashed, 13))
    hashed = hashed * jnp.int32(-1028477387)
    return hashed ^ lax.shift_right_logical(hashed, jnp.full_like(hashed, 16))


def gaussian(seed_value, counter):
    hashed = mix_hash(seed_value, counter)
    summed = jnp.bitwise_and(hashed, 255)
    summed = summed + jnp.bitwise_and(
        lax.shift_right_logical(hashed, jnp.full_like(hashed, 8)), 255
    )
    summed = summed + jnp.bitwise_and(
        lax.shift_right_logical(hashed, jnp.full_like(hashed, 16)), 255
    )
    summed = summed + lax.shift_right_logical(hashed, jnp.full_like(hashed, 24))
    return (summed - 510).astype(jnp.float32) / NOISE_SPREAD


def counter_grid(row_ids, group_ids, width, base):
    column_ids = jnp.arange(width, dtype=jnp.int32)
    return (
        base
        + (row_ids[:, None, None] * KV_HEADS + group_ids[None, :, None]) * width
        + column_ids[None, None, :]
    )


def rotary(vectors, cosine, sine_table):
    half_dim = vectors.shape[-1] // 2
    first_half = vectors[..., :half_dim]
    second_half = vectors[..., half_dim:]
    return jnp.concatenate(
        [
            first_half * cosine - second_half * sine_table,
            second_half * cosine + first_half * sine_table,
        ],
        axis=-1,
    )


def episode_tables(episode_row):
    count_rows = episode_row.shape[0]
    same_episode = episode_row[:, None] == episode_row[None, :]
    earlier = jnp.sum((episode_row[None, :] < episode_row[:, None]).astype(jnp.int32), axis=1)
    position = jnp.arange(count_rows, dtype=jnp.int32) - earlier
    causal = jnp.arange(count_rows)[None, :] <= jnp.arange(count_rows)[:, None]
    allowed = same_episode & causal
    frequency = jnp.exp(
        jnp.arange(0, HEAD_DIM, 2).astype(jnp.float32) * (-math.log(ROPE_BASE) / HEAD_DIM)
    )
    angles = position.astype(jnp.float32)[:, None] * frequency[None, :]
    return (allowed, jnp.cos(angles), jnp.sin(angles))


def on_device(
    tokens, episode, parent_index, mutation_seed, elite_project, elite_output, elite_bias
):
    child_rank = lax.axis_index("child")
    tensor_rank = lax.axis_index("tensor")
    kv_local = elite_project.shape[2]
    width_in = elite_project.shape[3]
    width_out = elite_output.shape[3]
    count_rows = tokens.shape[0]
    group_ids = tensor_rank * kv_local + jnp.arange(kv_local, dtype=jnp.int32)
    scale_in = MUTATION / math.sqrt(D)
    scale_out = MUTATION / math.sqrt(KV_HEADS * GROUP * HEAD_DIM)
    out_base = D * KV_HEADS * width_in
    bias_base = out_base + D * KV_HEADS * width_out
    own_seed = mutation_seed[0]
    parent = parent_index[child_rank]
    chosen_in = jnp.take(elite_project, parent_index, axis=0)
    chosen_out = jnp.take(elite_output, parent_index, axis=0)
    arrived_in, arrived_out = (
        lax.all_to_all(chosen_in, "child", split_axis=0, concat_axis=1, tiled=True),
        lax.all_to_all(chosen_out, "child", split_axis=0, concat_axis=1, tiled=True),
    )
    arrived_in = arrived_in[0]
    arrived_out = arrived_out[0]
    every_row = jnp.arange(D, dtype=jnp.int32)
    child_in = (
        arrived_in.astype(jnp.float32)
        + scale_in * gaussian(own_seed, counter_grid(every_row, group_ids, width_in, 0))
    ).astype(jnp.bfloat16)
    child_out = (
        arrived_out.astype(jnp.float32)
        + scale_out * gaussian(own_seed, counter_grid(every_row, group_ids, width_out, out_base))
    ).astype(jnp.bfloat16)
    counter_bias = (
        bias_base + group_ids[:, None] * width_in + jnp.arange(width_in, dtype=jnp.int32)[None, :]
    )
    child_bias = elite_bias[parent] + BIAS_MUTATION * gaussian(own_seed, counter_bias)
    projected = (
        jnp.einsum("rd,dgc->rgc", tokens, child_in, preferred_element_type=jnp.float32)
        + child_bias[None]
    )
    allowed, cosine, sine_table = episode_tables(episode[0])
    query_part = projected[:, :, : GROUP * HEAD_DIM].reshape(count_rows, kv_local, GROUP, HEAD_DIM)
    key_part = projected[:, :, GROUP * HEAD_DIM : (GROUP + 1) * HEAD_DIM]
    value_part = projected[:, :, (GROUP + 1) * HEAD_DIM :]
    queries = rotary(query_part, cosine[:, None, None, :], sine_table[:, None, None, :]).astype(
        jnp.bfloat16
    )
    key_rows = rotary(key_part, cosine[:, None, :], sine_table[:, None, :]).astype(jnp.bfloat16)
    values = value_part.astype(jnp.bfloat16)
    scores = jnp.einsum("rgqh,sgh->gqrs", queries, key_rows, preferred_element_type=jnp.float32) * (
        1.0 / math.sqrt(HEAD_DIM)
    )
    masked = jnp.where(allowed[None, None], scores, -jnp.inf)
    row_max = jnp.max(masked, axis=-1, keepdims=True)
    weights = jnp.exp(masked - row_max)
    probability = (weights / jnp.sum(weights, axis=-1, keepdims=True)).astype(jnp.bfloat16)
    context = jnp.einsum(
        "gqrs,sgh->rgqh", probability, values, preferred_element_type=jnp.float32
    ).astype(jnp.bfloat16)
    context = context.reshape(count_rows, kv_local, width_out)
    summed = lax.psum_scatter(
        jnp.einsum("dgc,rgc->dr", child_out, context, preferred_element_type=jnp.float32),
        "tensor",
        scatter_dimension=0,
        tiled=True,
    )
    return summed.T.astype(jnp.bfloat16)


def solution(mesh):
    in_specs = (
        P("child", None),
        P("child", None),
        P(),
        P("child"),
        P(None, "child", "tensor", None),
        P(None, "child", "tensor", None),
        P(None, "tensor", None),
    )
    out_specs = P("child", "tensor")
    return jax.shard_map(
        on_device, mesh=mesh, in_specs=in_specs, out_specs=out_specs, check_vma=False
    )
```

profile of v0, /device:TPU:1, one launch (start us, length us, event | category | flops | bytes accessed | tf_op | source)
XLA Modules:
  0.0 552.9 jit_solution(9426455333634282627)
XLA Ops:
  6.5 0.7 compare_select_fusion
  7.2 0.7 compare_and_fusion
  7.9 4.9 gather_fusion
  12.8 6.3 %bitcast_select_fusion.1 = bf16[64,80,1,640]{3,1,2,0:T(8,128)(2,1)} fusion(bf16[64,80,640]{2,1,0:T(8,128)(2,1)} %gather_fusion, pred[64]{0:T(512)(128)(4,1)S(1)} %compare_and_fusion), kind=kLoop, calls=%fused_computation.16 | loop fusion | flops 3276800 | bytes 13107264 | tf_op jit(solution)/shard_map/jit(_take)/select_n | solution.py:95
  19.1 15.3 %all-to-all-start = ((bf16[64,80,1,640]{3,1,2,0:T(8,128)(2,1)}), bf16[64,80,1,640]{3,1,2,0:T(8,128)(2,1)}, u32[]{:S(2)}, u32[]{:S(2)}) async-start(bf16[64,80,1,640]{3,1,2,0:T(8,128)(2,1)} %bitcast_select_fusion.1), calls=%async_computation | async-start | bytes 13107200 | tf_op jit(solution)/shard_map/all_to_all | solution.py:98
  34.5 5.9 %gather_fusion.1 = bf16[64,80,896]{2,1,0:T(8,128)(2,1)} fusion(bf16[2,80,896]{2,1,0:T(8,128)(2,1)S(1)} %bitcast.66, s32[1024]{0:T(1024)S(1)} %pad_clamp_fusion), kind=kCustom, calls=%fused_computation.1 | custom fusion | bytes 18350336 | tf_op jit(solution)/shard_map/jit(_take)/gather | solution.py:94
  40.4 8.1 %bitcast_select_fusion = bf16[64,80,1,896]{3,1,2,0:T(8,128)(2,1)} fusion(bf16[64,80,896]{2,1,0:T(8,128)(2,1)} %gather_fusion.1, pred[64]{0:T(512)(128)(4,1)S(1)} %compare_and_fusion), kind=kLoop, calls=%fused_computation.15 | loop fusion | flops 4587520 | bytes 18350144 | tf_op jit(solution)/shard_map/jit(_take)/select_n | solution.py:94
  48.5 125.0 %all-to-all-done = bf16[64,80,1,640]{3,1,2,0:T(8,128)(2,1)} async-done(((bf16[64,80,1,640]{3,1,2,0:T(8,128)(2,1)}), bf16[64,80,1,640]{3,1,2,0:T(8,128)(2,1)}, u32[]{:S(2)}, u32[]{:S(2)}) %all-to-all-start) | async-done | bytes 6553632 | tf_op jit(solution)/shard_map/all_to_all | solution.py:98
  173.6 14.8 %all-to-all-start.1 = ((bf16[64,80,1,896]{3,1,2,0:T(8,128)(2,1)}), bf16[64,80,1,896]{3,1,2,0:T(8,128)(2,1)}, u32[]{:S(2)}, u32[]{:S(2)}) async-start(bf16[64,80,1,896]{3,1,2,0:T(8,128)(2,1)} %bitcast_select_fusion), calls=%async_computation.1 | async-start | bytes 18350080 | tf_op jit(solution)/shard_map/all_to_all | solution.py:97
  192.4 1.0 multiply_cosine_fusion
  193.4 14.2 %add_convert_fusion = bf16[64,80,1,640]{3,1,2,0:T(8,128)(2,1)} fusion(bf16[64,80,1,640]{3,1,2,0:T(8,128)(2,1)} %all-to-all-done, s32[]{:T(128)} %bitcast.2, s32[64,80]{1,0:T(8,128)S(1)} %multiply_add_fusion), kind=kLoop, calls=%fused_computation.14 | loop fusion | flops 81920000 | bytes 13127684 | tf_op jit(solution)/shard_map/convert_element_type | solution.py:110
  207.5 177.1 %all-to-all-done.1 = bf16[64,80,1,896]{3,1,2,0:T(8,128)(2,1)} async-done(((bf16[64,80,1,896]{3,1,2,0:T(8,128)(2,1)}), bf16[64,80,1,896]{3,1,2,0:T(8,128)(2,1)}, u32[]{:S(2)}, u32[]{:S(2)}) %all-to-all-start.1) | async-done | bytes 9175072 | tf_op jit(solution)/shard_map/all_to_all | solution.py:97
  384.6 18.2 %fusion.2 = bf16[5120,896]{1,0:T(8,128)(2,1)S(1)} fusion(bf16[64,80,1,896]{3,1,2,0:T(8,128)(2,1)} %all-to-all-done.1, s32[]{:T(128)} %bitcast.2, s32[5120]{0:T(1024)S(1)} %add_multiply_fusion), kind=kLoop, calls=%fused_computation.11 | loop fusion | flops 114688000 | bytes 18370564 | tf_op jit(solution)/shard_map/convert_element_type | solution.py:106
  402.9 8.2 %add_bitcast_fusion = f32[512,1,896]{0,2,1:T(8,128)S(1)} fusion(bf16[5120,896]{1,0:T(8,128)(2,1)S(1)} %fusion.2, bf16[512,5120]{1,0:T(8,128)(2,1)} %param.7, f32[896]{0:T(1024)S(1)} %add_reduce_fusion), kind=kOutput, calls=%fused_computation.25 | convolution fusion | flops 4698079232 | bytes 16256512 | tf_op jit(solution)/shard_map/rd,dgc->rgc/dot_general | solution.py:116
  411.2 1.2 fusion.33
  412.4 1.0 fusion.39
  413.7 1.5 copy.22
  415.6 2.3 fusion.6
  417.9 1.1 fusion.5
  419.0 2.9 fusion.10
  421.9 6.8 %fusion.40 = f32[5120,512]{1,0:T(8,128)} fusion(bf16[5120,640]{1,0:T(8,128)(2,1)S(1)} %bitcast.70, bf16[512,640]{0,1:T(8,128)(2,1)S(1)} %bitcast.74), kind=kOutput, calls=%fused_computation.75 | convolution fusion | flops 3355443200 | bytes 17694720 | tf_op jit(solution)/shard_map/dgc,rgc->dr/dot_general | solution.py:140
  428.7 113.9 %reduce-scatter.2.cloned.1.call-done = f32[1280,512]{1,0:T(8,128)} async-done(((f32[5120,512]{1,0:T(8,128)}), f32[1280,512]{1,0:T(8,128)}) %reduce-scatter.2.cloned.1.call-update) | async-done | bytes 2621456 | tf_op jit(solution)/shard_map/reduce_scatter | solution.py:139
  542.6 1.9 convert_bitcast_fusion
  544.6 1.4 copy.17
  (31 shorter events, 2.2 us)
Async XLA Ops:
  6.5 27.9 %copy-start = (bf16[2,80,1,896]{3,1,2,0:T(8,128)(2,1)S(1)}, bf16[2,80,1,896]{3,1,2,0:T(8,128)(2,1)}, u32[]{:S(2)}) copy-start(bf16[2,80,1,896]{3,1,2,0:T(8,128)(2,1)} %param.11) | copy-start | bytes 860164
  19.1 154.5 %all-to-all-start = ((bf16[64,80,1,640]{3,1,2,0:T(8,128)(2,1)}), bf16[64,80,1,640]{3,1,2,0:T(8,128)(2,1)}, u32[]{:S(2)}, u32[]{:S(2)}) async-start(bf16[64,80,1,640]{3,1,2,0:T(8,128)(2,1)} %bitcast_select_fusion.1), calls=%async_computation | async-start | bytes 13107200 | tf_op jit(solution)/shard_map/all_to_all | solution.py:98
  48.5 140.1 %copy-start.5 = (s32[64]{0:T(128)S(1)}, s32[64]{0:T(128)}, u32[]{:S(2)}) copy-start(s32[64]{0:T(128)} %param.9) | copy-start | bytes 772
  48.5 143.3 %copy-start.4 = (f32[2,1,896]{2,1,0:T(1,128)S(1)}, f32[2,1,896]{2,1,0:T(1,128)}, u32[]{:S(2)}) copy-start(f32[2,1,896]{2,1,0:T(1,128)} %param.13) | copy-start | bytes 21508
  48.5 143.4 %copy-start.3 = (s32[1,512]{1,0:T(1,128)S(1)}, s32[1,512]{1,0:T(1,128)}, u32[]{:S(2)}) copy-start(s32[1,512]{1,0:T(1,128)} %param.8) | copy-start | bytes 6148
  173.6 211.0 %all-to-all-start.1 = ((bf16[64,80,1,896]{3,1,2,0:T(8,128)(2,1)}), bf16[64,80,1,896]{3,1,2,0:T(8,128)(2,1)}, u32[]{:S(2)}, u32[]{:S(2)}) async-start(bf16[64,80,1,896]{3,1,2,0:T(8,128)(2,1)} %bitcast_select_fusion), calls=%async_computation.1 | async-start | bytes 18350080 | tf_op jit(solution)/shard_map/all_to_all | solution.py:97
  188.4 354.2 %reduce-scatter.2.cloned.1.call-start = ((), (), s32[]{:S(2)}) async-start(), calls=%async_computation.3 | async-start | bytes 13107200 | tf_op jit(solution)/shard_map/reduce_scatter | solution.py:139
  411.1 2.3 copy-start.2
  417.9 4.0 slice-start
  419.0 2.9 slice-start.1
  421.9 124.1 %copy-start.1 = (bf16[2,80,1,896]{3,1,2,0:T(8,128)(2,1)S(1)}, bf16[2,80,1,896]{3,1,2,0:T(8,128)(2,1)}, u32[]{:S(2)}) copy-start(bf16[2,80,1,896]{3,1,2,0:T(8,128)(2,1)} %param.11) | copy-start | bytes 860164
Sparse Core Ops, SparseCore 0:
  428.9 113.7 reduce-scatter.1
where the time goes:
time: 553 us
  waiting for transfers between devices  416 us (75%)
  other arithmetic  54.2 us (10%)
  starting transfers between devices  30.4 us (5%)
  matrix products  20.1 us (4%)
  between operations  16.2 us (3%)
  local copies, waits for them, and re-layouts  15.9 us (3%)
    all_to_all x1, waiting for transfers between devices, on_device(): lax.all_to_all(chosen_in, 'child', split_axis=0, concat_axis=1, tiled=True)  177 us
    all_to_all x1, waiting for transfers between devices, on_device(): lax.all_to_all(chosen_out, 'child', split_axis=0, concat_axis=1, tiled=True)  125 us
    reduce_scatter x1, waiting for transfers between devices, on_device(): lax.psum_scatter(jnp.einsum('dgc,rgc->dr', child_out, context, preferred_...  114 us
    convert_element_type x1, other arithmetic, on_device(): child_in = (arrived_in.astype(jnp.float32) + scale_in * gaussian(own_seed...  18.2 us
    all_to_all x1, starting transfers between devices, on_device(): lax.all_to_all(chosen_out, 'child', split_axis=0, concat_axis=1, tiled=True)  15.3 us
    all_to_all x1, starting transfers between devices, on_device(): lax.all_to_all(chosen_in, 'child', split_axis=0, concat_axis=1, tiled=True)  14.8 us
    convert_element_type x1, other arithmetic, on_device(): child_out = (arrived_out.astype(jnp.float32) + scale_out * gaussian(own_s...  14.2 us
  transfers between devices with their start and end apart: 3, of which 3 were waited for; matrix products, arithmetic and copies ran while one was open for 5% of the time, Pallas kernels for 0%

commit v1 on v0

--- a/solution.py
+++ b/solution.py
@@ -91,14 +91,10 @@
     bias_base = out_base + D * KV_HEADS * width_out
     own_seed = mutation_seed[0]
     parent = parent_index[child_rank]
-    chosen_in = jnp.take(elite_project, parent_index, axis=0)
-    chosen_out = jnp.take(elite_output, parent_index, axis=0)
-    arrived_in, arrived_out = (
-        lax.all_to_all(chosen_in, "child", split_axis=0, concat_axis=1, tiled=True),
-        lax.all_to_all(chosen_out, "child", split_axis=0, concat_axis=1, tiled=True),
-    )
-    arrived_in = arrived_in[0]
-    arrived_out = arrived_out[0]
+    gathered_in = lax.all_gather(elite_project, "child", axis=1, tiled=True)
+    gathered_out = lax.all_gather(elite_output, "child", axis=1, tiled=True)
+    arrived_in = lax.dynamic_index_in_dim(gathered_in, parent, 0, keepdims=False)
+    arrived_out = lax.dynamic_index_in_dim(gathered_out, parent, 0, keepdims=False)
     every_row = jnp.arange(D, dtype=jnp.int32)
     child_in = (
         arrived_in.astype(jnp.float32)

time: 553 us -> 466 us (0.84)
  other arithmetic: 54.2 us -> 11 us
  starting transfers between devices: 30.4 us -> 0.08 us
  waiting for transfers between devices: 416 us -> 391 us
  matrix products: 20.1 us -> 43.1 us
  local copies, waits for them, and re-layouts: 15.9 us -> 4.72 us
    all_to_all x2 -> x0, waiting for transfers between devices: 302 us -> none  [the longest x1 177 us: on_device(): lax.all_to_all(chosen_in, 'child', split_axis=0, concat_axis=1, tiled=True)]
    all_gather x0 -> x2, waiting for transfers between devices: none -> 285 us  [the longest x1 167 us: on_device(): gathered_in = lax.all_gather(elite_project, 'child', axis=1, tiled=True)]
    convert_element_type x2 -> x0, other arithmetic: 32.4 us -> none  [the longest x1 18.2 us: on_device(): child_in = (arrived_in.astype(jnp.float32) + scale_in * gaussian(own_seed...]
    all_to_all x2 -> x0, starting transfers between devices: 30.2 us -> none  [the longest x1 15.3 us: on_device(): lax.all_to_all(chosen_out, 'child', split_axis=0, concat_axis=1, tiled=True)]
    dot_general x1, matrix products: 8.17 us -> 23.9 us  [on_device(): jnp.einsum('rd,dgc->rgc', tokens, child_in, preferred_element_type=jnp.fl...]
    select_n x3 -> x0, other arithmetic: 15.1 us -> none  [the longest x1 8.14 us: on_device(): chosen_in = jnp.take(elite_project, parent_index, axis=0)]
    gather x2 -> x0, local copies, waits for them, and re-layouts: 10.9 us -> none  [the longest x1 5.94 us: on_device(): chosen_in = jnp.take(elite_project, parent_index, axis=0)]
    reduce_scatter x1, waiting for transfers between devices: 114 us -> 105 us  [on_device(): lax.psum_scatter(jnp.einsum('dgc,rgc->dr', child_out, context, preferred_...]
  transfers between devices with their start and end apart: 3 -> 3, of which waited for: 3 -> 3; matrix products, arithmetic and copies ran while one was open for 5% -> 8% of each run, Pallas kernels for 0% -> 0%
where the time goes in v1:
time: 466 us
  waiting for transfers between devices  391 us (84%)
  matrix products  43.1 us (9%)
  between operations  15.8 us (3%)
  other arithmetic  11 us (2%)
  local copies, waits for them, and re-layouts  4.72 us (1%)
    all_gather x1, waiting for transfers between devices, on_device(): gathered_in = lax.all_gather(elite_project, 'child', axis=1, tiled=True)  167 us
    all_gather x1, waiting for transfers between devices, on_device(): gathered_out = lax.all_gather(elite_output, 'child', axis=1, tiled=True)  118 us
    reduce_scatter x1, waiting for transfers between devices, on_device(): lax.psum_scatter(jnp.einsum('dgc,rgc->dr', child_out, context, preferred_...  105 us
    dot_general x1, matrix products, on_device(): jnp.einsum('rd,dgc->rgc', tokens, child_in, preferred_element_type=jnp.fl...  23.9 us
    dot_general x1, matrix products, on_device(): jnp.einsum('dgc,rgc->dr', child_out, context, preferred_element_type=jnp....  15.1 us
  transfers between devices with their start and end apart: 3, of which 3 were waited for; matrix products, arithmetic and copies ran while one was open for 8% of the time, Pallas kernels for 0%

profile of v1, /device:TPU:1, one launch (start us, length us, event | category | flops | bytes accessed | tf_op | source)
XLA Modules:
  0.0 466.1 jit_solution(12273178524650003654)
XLA Ops:
  6.5 0.7 all-gather.5.cloned.1.call-update
  7.3 0.7 all-gather.3.cloned.1.call-update
  8.1 1.2 dynamic_slice.14
  11.9 0.7 add_reduce_fusion
  12.7 0.6 multiply_add_fusion
  13.3 0.9 convert_reduce_fusion
  14.2 1.0 fusion.20
  15.2 1.8 multiply_cosine_fusion
  17.0 166.9 %all-gather.5.cloned.1.call-done = bf16[2,5120,1,896]{3,1,2,0:T(8,128)(2,1)} async-done(((bf16[2,80,1,896]{3,1,2,0:T(8,128)(2,1)}), bf16[2,5120,1,896]{3,1,2,0:T(8,128)(2,1)}) %all-gather.5.cloned.1.call-update) | async-done | bytes 18350096 | tf_op jit(solution)/shard_map/all_gather | solution.py:94
  183.9 23.9 %add_bitcast_fusion = f32[512,1,896]{0,2,1:T(8,128)S(1)} fusion(bf16[512,5120]{1,0:T(8,128)(2,1)} %param.7, s32[]{:T(128)} %bitcast.1, s32[5120]{0:T(1024)S(1)} %fusion.41, bf16[2,5120,1,896]{3,1,2,0:T(8,128)(2,1)} %all-gather.5.cloned.1.call-done, s32[]{:T(128)S(6)} %select_n.15, f32[896]{0:T(1024)S(1)} %add_reduce_fusion), kind=kOutput, calls=%fused_computation.24 | convolution fusion | flops 4812767232 | bytes 16277508 | tf_op jit(solution)/shard_map/rd,dgc->rgc/dot_general | solution.py:112
  207.9 0.1 fusion.67
  208.0 1.0 copy-done
  209.0 0.4 copy.16
  209.4 0.4 copy.17
  209.9 1.5 fusion.40
  211.4 1.4 fusion.21
  212.8 1.4 fusion.11
  214.2 1.1 fusion.10
  215.3 2.7 fusion.17
  218.0 117.9 %all-gather.3.cloned.1.call-done = bf16[2,5120,1,640]{3,1,2,0:T(8,128)(2,1)} async-done(((bf16[2,80,1,640]{3,1,2,0:T(8,128)(2,1)}), bf16[2,5120,1,640]{3,1,2,0:T(8,128)(2,1)}) %all-gather.3.cloned.1.call-update) | async-done | bytes 13107216 | tf_op jit(solution)/shard_map/all_gather | solution.py:95
  335.9 15.1 %fusion.8 = f32[5120,512]{1,0:T(8,128)} fusion(bf16[512,640]{0,1:T(8,128)(2,1)S(1)} %bitcast.66, s32[]{:T(128)} %bitcast.1, s32[5120]{0:T(1024)S(1)} %copy-done.1, bf16[2,5120,1,640]{3,1,2,0:T(8,128)(2,1)} %all-gather.3.cloned.1.call-done, s32[]{:T(128)S(6)} %select_n.15), kind=kOutput, calls=%fused_computation.15 | convolution fusion | flops 3437363200 | bytes 17715716 | tf_op jit(solution)/shard_map/dgc,rgc->dr/dot_general | solution.py:136
  351.0 105.2 %reduce-scatter.2.cloned.1.call-done = f32[1280,512]{1,0:T(8,128)} async-done(((f32[5120,512]{1,0:T(8,128)}), f32[1280,512]{1,0:T(8,128)}) %reduce-scatter.2.cloned.1.call-update) | async-done | bytes 2621456 | tf_op jit(solution)/shard_map/reduce_scatter | solution.py:135
  456.2 1.9 convert_bitcast_fusion
  458.1 1.4 copy.12
  (11 shorter events, 0.2 us)
Async XLA Ops:
  6.5 177.3 %all-gather.5.cloned.1.call-start = ((), (), s32[]{:S(2)}) async-start(), calls=%async_computation.2 | async-start | bytes 18636800 | tf_op jit(solution)/shard_map/all_gather | solution.py:94
  7.3 328.7 %all-gather.3.cloned.1.call-start = ((), (), s32[]{:S(2)}) async-start(), calls=%async_computation.1 | async-start | bytes 13312000 | tf_op jit(solution)/shard_map/all_gather | solution.py:95
  8.0 448.2 %reduce-scatter.2.cloned.1.call-start = ((), (), s32[]{:S(2)}) async-start(), calls=%async_computation.3 | async-start | bytes 13107200 | tf_op jit(solution)/shard_map/reduce_scatter | solution.py:135
  207.8 1.3 copy-start
  215.3 120.6 %copy-start.1 = (s32[5120]{0:T(1024)S(1)}, s32[5120]{0:T(1024)}, u32[]{:S(2)}) copy-start(s32[5120]{0:T(1024)} %multiply_add_fusion) | copy-start | bytes 61444
Sparse Core Ops, SparseCore 0:
  10.7 173.1 all-gather.4
  187.2 148.6 all-gather.2
  351.2 104.9 reduce-scatter.1

commit v2 on v1

--- a/solution.py
+++ b/solution.py
@@ -75,11 +75,40 @@
     return (allowed, jnp.cos(angles), jnp.sin(angles))
 
 
+def output_rows(elite_output, parent_index, child_count, tensor_count, gather_rows):
+    local_rows = elite_output.shape[1]
+    every_group = lax.all_gather(elite_output, "tensor", axis=2, tiled=True)
+    span = child_count // tensor_count
+    piece = local_rows // tensor_count
+    pairs = []
+    for source_child in range(child_count):
+        for part in range(tensor_count):
+            target_child = tensor_count * (source_child % span) + part
+            target_tensor = source_child // span
+            pairs.append(
+                (source_child * tensor_count + part, target_child * tensor_count + target_tensor)
+            )
+    tensor_rank = lax.axis_index("tensor")
+    mine = lax.dynamic_slice_in_dim(every_group, tensor_rank * piece, piece, axis=1)
+    shuffled = lax.ppermute(mine, ("child", "tensor"), pairs)
+    if gather_rows:
+        gathered = lax.all_gather(shuffled, "child", axis=1, tiled=True)
+        parent = parent_index[lax.axis_index("child")]
+        return lax.dynamic_index_in_dim(gathered, parent, 0, keepdims=False)
+    chosen = jnp.take(shuffled, parent_index, axis=0)
+    return lax.all_to_all(chosen, "child", split_axis=0, concat_axis=1, tiled=True)[0]
+
+
+GATHER_OUTPUT_ROWS = False
+
+
 def on_device(
     tokens, episode, parent_index, mutation_seed, elite_project, elite_output, elite_bias
 ):
     child_rank = lax.axis_index("child")
     tensor_rank = lax.axis_index("tensor")
+    child_count = lax.axis_size("child")
+    tensor_count = lax.axis_size("tensor")
     kv_local = elite_project.shape[2]
     width_in = elite_project.shape[3]
     width_out = elite_output.shape[3]
@@ -92,17 +121,21 @@
     own_seed = mutation_seed[0]
     parent = parent_index[child_rank]
     gathered_in = lax.all_gather(elite_project, "child", axis=1, tiled=True)
-    gathered_out = lax.all_gather(elite_output, "child", axis=1, tiled=True)
     arrived_in = lax.dynamic_index_in_dim(gathered_in, parent, 0, keepdims=False)
-    arrived_out = lax.dynamic_index_in_dim(gathered_out, parent, 0, keepdims=False)
+    arrived_out = output_rows(
+        elite_output, parent_index, child_count, tensor_count, GATHER_OUTPUT_ROWS
+    )
     every_row = jnp.arange(D, dtype=jnp.int32)
     child_in = (
         arrived_in.astype(jnp.float32)
         + scale_in * gaussian(own_seed, counter_grid(every_row, group_ids, width_in, 0))
     ).astype(jnp.bfloat16)
+    out_rows = arrived_out.shape[0]
+    own_rows = tensor_rank * out_rows + jnp.arange(out_rows, dtype=jnp.int32)
+    all_groups = jnp.arange(KV_HEADS, dtype=jnp.int32)
     child_out = (
         arrived_out.astype(jnp.float32)
-        + scale_out * gaussian(own_seed, counter_grid(every_row, group_ids, width_out, out_base))
+        + scale_out * gaussian(own_seed, counter_grid(own_rows, all_groups, width_out, out_base))
     ).astype(jnp.bfloat16)
     counter_bias = (
         bias_base + group_ids[:, None] * width_in + jnp.arange(width_in, dtype=jnp.int32)[None, :]
@@ -132,13 +165,11 @@
         "gqrs,sgh->rgqh", probability, values, preferred_element_type=jnp.float32
     ).astype(jnp.bfloat16)
     context = context.reshape(count_rows, kv_local, width_out)
-    summed = lax.psum_scatter(
-        jnp.einsum("dgc,rgc->dr", child_out, context, preferred_element_type=jnp.float32),
-        "tensor",
-        scatter_dimension=0,
-        tiled=True,
+    every_context = lax.all_gather(context, "tensor", axis=1, tiled=True)
+    attended = jnp.einsum(
+        "rgc,dgc->rd", every_context, child_out, preferred_element_type=jnp.float32
     )
-    return summed.T.astype(jnp.bfloat16)
+    return attended.astype(jnp.bfloat16)
 
 
 def solution(mesh):

time: 466 us -> 433 us (0.929)
  waiting for transfers between devices: 391 us -> 285 us
  starting transfers between devices: 0.08 us -> 39.7 us
  other arithmetic: 11 us -> 25 us
  blocking collectives: 0 us -> 10.7 us
  local copies, waits for them, and re-layouts: 4.72 us -> 12.7 us
    reduce_scatter x1 -> x0, waiting for transfers between devices: 105 us -> none  [on_device(): lax.psum_scatter(jnp.einsum('dgc,rgc->dr', child_out, context, preferred_...]
    all_gather x1, waiting for transfers between devices: 118 us -> 48.5 us  [on_device(): every_context = lax.all_gather(context, 'tensor', axis=1, tiled=True)]
    all_gather x1, waiting for transfers between devices: 167 us -> 231 us  [on_device(): gathered_in = lax.all_gather(elite_project, 'child', axis=1, tiled=True)]
    all_to_all x0 -> x1, starting transfers between devices: none -> 36.4 us  [output_rows(): lax.all_to_all(chosen, 'child', split_axis=0, concat_axis=1, tiled=True)[0]]
    all_gather x0 -> x1, blocking collectives: none -> 10.7 us  [output_rows(): every_group = lax.all_gather(elite_output, 'tensor', axis=2, tiled=True)]
    select_n x0 -> x2, other arithmetic: none -> 9.25 us  [output_rows(): chosen = jnp.take(shuffled, parent_index, axis=0)]
    gather x0 -> x1, local copies, waits for them, and re-layouts: none -> 8.9 us  [output_rows(): chosen = jnp.take(shuffled, parent_index, axis=0)]
    convert_element_type x1, other arithmetic: 1.91 us -> 8.81 us  [on_device(): arrived_out.astype(jnp.float32)]
  transfers between devices with their start and end apart: 3 -> 4, of which waited for: 3 -> 3; matrix products, arithmetic and copies ran while one was open for 8% -> 15% of each run, Pallas kernels for 0% -> 0%
where the time goes in v2:
time: 433 us
  waiting for transfers between devices  285 us (66%)
  matrix products  43.6 us (10%)
  starting transfers between devices  39.7 us (9%)
  other arithmetic  25 us (6%)
  between operations  16.2 us (4%)
  local copies, waits for them, and re-layouts  12.7 us (3%)
  blocking collectives  10.7 us (2%)
    all_gather x1, waiting for transfers between devices, on_device(): gathered_in = lax.all_gather(elite_project, 'child', axis=1, tiled=True)  231 us
    all_gather x1, waiting for transfers between devices, on_device(): every_context = lax.all_gather(context, 'tensor', axis=1, tiled=True)  48.5 us
    all_to_all x1, starting transfers between devices, output_rows(): lax.all_to_all(chosen, 'child', split_axis=0, concat_axis=1, tiled=True)[0]  36.4 us
    dot_general x1, matrix products, on_device(): jnp.einsum('rd,dgc->rgc', tokens, child_in, preferred_element_type=jnp.fl...  23.9 us
    dot_general x1, matrix products, on_device(): jnp.einsum('rgc,dgc->rd', every_context, child_out, preferred_element_typ...  15.6 us
    all_gather x1, blocking collectives, output_rows(): every_group = lax.all_gather(elite_output, 'tensor', axis=2, tiled=True)  10.7 us
    select_n x2, other arithmetic, output_rows(): chosen = jnp.take(shuffled, parent_index, axis=0)  9.25 us
    gather x1, local copies, waits for them, and re-layouts, output_rows(): chosen = jnp.take(shuffled, parent_index, axis=0)  8.9 us
  transfers between devices with their start and end apart: 4, of which 3 were waited for; matrix products, arithmetic and copies ran while one was open for 15% of the time, Pallas kernels for 0%

profile of v2, /device:TPU:1, one launch (start us, length us, event | category | flops | bytes accessed | tf_op | source)
XLA Modules:
  0.0 432.6 jit_solution(5225770503054642974)
XLA Ops:
  6.5 0.7 all-gather.3.cloned.1.call-update
  7.3 10.7 %all_gather.11 = bf16[2,80,4,640]{3,1,0,2:T(8,128)(2,1)S(1)} all-gather(bf16[2,80,1,640]{3,1,0,2:T(8,128)(2,1)} %bitcast.68), channel_id=1, replica_groups=mesh['child'=64,'tensor'=4] {'tensor'}, dimensions={2}, use_global_device_ids=true | all-gather | bytes 1024000 | tf_op jit(solution)/shard_map/all_gather | solution.py:80
  18.2 3.2 collective-permute-start
  21.4 0.7 compare_select_fusion
  22.1 0.7 compare_and_fusion
  22.8 4.3 %collective-permute-done = bf16[2,20,4,640]{3,2,1,0:T(4,128)(2,1)S(1)} collective-permute-done((bf16[2,20,4,640]{3,2,1,0:T(4,128)(2,1)S(1)}, bf16[2,20,4,640]{3,2,1,0:T(4,128)(2,1)S(1)}, u32[]{:S(2)}, u32[]{:S(2)}) %collective-permute-start) | collective-permute-done | bytes 204832 | tf_op jit(solution)/shard_map/ppermute | solution.py:93
  27.1 8.9 %gather_fusion = bf16[64,20,4,640]{3,2,1,0:T(4,128)(2,1)} fusion(bf16[2,20,4,640]{3,2,1,0:T(4,128)(2,1)S(1)} %collective-permute-done, s32[1024]{0:T(1024)S(1)} %pad_clamp_fusion), kind=kCustom, calls=%fused_computation | custom fusion | bytes 13107456 | tf_op jit(solution)/shard_map/jit(_take)/gather | solution.py:98
  36.0 8.6 %broadcast_select_fusion = bf16[64,20,4,640]{3,2,1,0:T(4,128)(2,1)} fusion(bf16[64,20,4,640]{3,2,1,0:T(4,128)(2,1)} %gather_fusion, pred[64]{0:T(512)(128)(4,1)S(1)} %compare_and_fusion), kind=kLoop, calls=%fused_computation.17 | loop fusion | flops 3276800 | bytes 13107264 | tf_op jit(solution)/shard_map/jit(_take)/select_n | solution.py:98
  44.6 36.4 %all-to-all-start = ((bf16[64,20,4,640]{3,2,1,0:T(4,128)(2,1)}), bf16[64,20,4,640]{3,2,1,0:T(4,128)(2,1)}, u32[]{:S(2)}, u32[]{:S(2)}) async-start(bf16[64,20,4,640]{3,2,1,0:T(4,128)(2,1)} %broadcast_select_fusion), calls=%async_computation | async-start | bytes 13107200 | tf_op jit(solution)/shard_map/all_to_all | solution.py:99
  81.1 0.6 dynamic_slice.13
  84.8 1.8 multiply_cosine_fusion
  86.6 231.1 %all-gather.3.cloned.1.call-done = bf16[2,5120,1,896]{3,1,2,0:T(8,128)(2,1)} async-done(((bf16[2,80,1,896]{3,1,2,0:T(8,128)(2,1)}), bf16[2,5120,1,896]{3,1,2,0:T(8,128)(2,1)}) %all-gather.3.cloned.1.call-update) | async-done | bytes 18350096 | tf_op jit(solution)/shard_map/all_gather | solution.py:123
  317.7 23.9 %add_bitcast_fusion = f32[512,1,896]{0,2,1:T(8,128)S(1)} fusion(bf16[512,5120]{1,0:T(8,128)(2,1)} %param.7, s32[]{:T(128)} %bitcast.2, s32[5120]{0:T(1024)S(1)} %add_multiply_fusion, bf16[2,5120,1,896]{3,1,2,0:T(8,128)(2,1)} %all-gather.3.cloned.1.call-done, s32[]{:T(128)S(6)} %select_n.25, f32[896]{0:T(1024)S(1)} %add_reduce_fusion), kind=kOutput, calls=%fused_computation.29 | convolution fusion | flops 4812767232 | bytes 16277508 | tf_op jit(solution)/shard_map/rd,dgc->rgc/dot_general | solution.py:145
  341.8 1.0 copy-done
  343.3 0.4 copy.53
  343.7 1.5 fusion.46
  345.2 1.4 fusion.27
  346.6 1.4 fusion.11
  348.0 1.1 fusion.10
  349.1 2.6 fusion.23
  351.8 1.1 copy.45
  352.9 8.8 %bitcast_convert_fusion = f32[1280,4,640]{2,1,0:T(4,128)} fusion(bf16[64,20,4,640]{3,2,1,0:T(4,128)(2,1)} %all-to-all-done), kind=kLoop, calls=%fused_computation.16 | loop fusion | flops 3276800 | bytes 19660800 | tf_op jit(solution)/shard_map/convert_element_type | solution.py:137
  361.7 48.5 %all-gather.5.cloned.1.call-done = bf16[512,4,640]{2,0,1:T(8,128)(2,1)} async-done(((bf16[512,1,640]{2,0,1:T(8,128)(2,1)}), bf16[512,4,640]{2,0,1:T(8,128)(2,1)}) %all-gather.5.cloned.1.call-update) | async-done | bytes 2621456 | tf_op jit(solution)/shard_map/all_gather | solution.py:168
  410.2 15.6 %fusion.15 = bf16[512,1280]{1,0:T(8,128)(2,1)} fusion(bf16[512,4,640]{2,0,1:T(8,128)(2,1)} %all-gather.5.cloned.1.call-done, f32[1280,4,640]{2,1,0:T(4,128)} %bitcast_convert_fusion, s32[]{:T(128)} %bitcast.2, s32[1280,4]{0,1:T(4,128)S(1)} %multiply_add_fusion), kind=kOutput, calls=%fused_computation.25 | convolution fusion | flops 3434741760 | bytes 17059844 | tf_op jit(solution)/shard_map/rgc,dgc->rd/dot_general | solution.py:169
  (25 shorter events, 1.3 us)
Async XLA Ops:
  6.5 311.1 %all-gather.3.cloned.1.call-start = ((), (), s32[]{:S(2)}) async-start(), calls=%async_computation.1 | async-start | bytes 18636800 | tf_op jit(solution)/shard_map/all_gather | solution.py:123
  18.2 8.9 %collective-permute-start = (bf16[2,20,4,640]{3,2,1,0:T(4,128)(2,1)S(1)}, bf16[2,20,4,640]{3,2,1,0:T(4,128)(2,1)S(1)}, u32[]{:S(2)}, u32[]{:S(2)}) collective-permute-start(bf16[2,20,4,640]{3,2,1,0:T(4,128)(2,1)S(1)} %copy.54), channel_id=1, source_target_pairs={{0,0},{1,4},{2,8},{3,12},{4,16},{5,20},{6,24},{7,28},{8,32},{9,36}... | collective-permute-start | bytes 614408 | tf_op jit(solution)/shard_map/ppermute | solution.py:93
  44.6 36.5 %copy-start.3 = (s32[64]{0:T(128)S(1)}, s32[64]{0:T(128)}, u32[]{:S(2)}) copy-start(s32[64]{0:T(128)} %param.9) | copy-start | bytes 772
  44.6 39.7 %copy-start.2 = (f32[2,1,896]{2,1,0:T(1,128)S(1)}, f32[2,1,896]{2,1,0:T(1,128)}, u32[]{:S(2)}) copy-start(f32[2,1,896]{2,1,0:T(1,128)} %param.13) | copy-start | bytes 21508
  44.6 39.8 %copy-start.1 = (s32[1,512]{1,0:T(1,128)S(1)}, s32[1,512]{1,0:T(1,128)}, u32[]{:S(2)}) copy-start(s32[1,512]{1,0:T(1,128)} %param.8) | copy-start | bytes 6148
  44.6 308.3 %all-to-all-start = ((bf16[64,20,4,640]{3,2,1,0:T(4,128)(2,1)}), bf16[64,20,4,640]{3,2,1,0:T(4,128)(2,1)}, u32[]{:S(2)}, u32[]{:S(2)}) async-start(bf16[64,20,4,640]{3,2,1,0:T(4,128)(2,1)} %broadcast_select_fusion), calls=%async_computation | async-start | bytes 13107200 | tf_op jit(solution)/shard_map/all_to_all | solution.py:99
  81.0 329.2 %all-gather.5.cloned.1.call-start = ((), (), s32[]{:S(2)}) async-start(), calls=%async_computation.2 | async-start | bytes 3276800 | tf_op jit(solution)/shard_map/all_gather | solution.py:168
  341.6 1.2 copy-start
Sparse Core Ops, SparseCore 0:
  10.7 306.9 all-gather.2
  353.0 57.1 all-gather.4

commit v3 on v2

--- a/solution.py
+++ b/solution.py
@@ -99,7 +99,7 @@
     return lax.all_to_all(chosen, "child", split_axis=0, concat_axis=1, tiled=True)[0]
 
 
-GATHER_OUTPUT_ROWS = False
+GATHER_OUTPUT_ROWS = True
 
 
 def on_device(

time: 433 us -> 424 us (0.979)
  waiting for transfers between devices: 285 us -> 328 us
  starting transfers between devices: 39.7 us -> 3.33 us
  other arithmetic: 25 us -> 8.51 us
    all_gather x0 -> x1, waiting for transfers between devices: none -> 113 us  [output_rows(): gathered = lax.all_gather(shuffled, 'child', axis=1, tiled=True)]
    all_gather x1, waiting for transfers between devices: 231 us -> 168 us  [on_device(): gathered_in = lax.all_gather(elite_project, 'child', axis=1, tiled=True)]
    all_to_all x1 -> x0, starting transfers between devices: 36.4 us -> none  [output_rows(): lax.all_to_all(chosen, 'child', split_axis=0, concat_axis=1, tiled=True)[0]]
    all_gather x1, waiting for transfers between devices: 48.5 us -> 38.9 us  [on_device(): every_context = lax.all_gather(context, 'tensor', axis=1, tiled=True)]
    select_n x2 -> x0, other arithmetic: 9.25 us -> none  [output_rows(): chosen = jnp.take(shuffled, parent_index, axis=0)]
    gather x1 -> x0, local copies, waits for them, and re-layouts: 8.9 us -> none  [output_rows(): chosen = jnp.take(shuffled, parent_index, axis=0)]
    convert_element_type x1 -> x0, other arithmetic: 8.81 us -> none  [on_device(): arrived_out.astype(jnp.float32)]
    dynamic_slice x0 -> x1, local copies, waits for them, and re-layouts: none -> 7.88 us  [output_rows(): return lax.dynamic_index_in_dim(gathered, parent, 0, keepdims=False)]
  transfers between devices with their start and end apart: 4 -> 4, of which waited for: 3 -> 4; matrix products, arithmetic and copies ran while one was open for 15% -> 11% of each run, Pallas kernels for 0% -> 0%
where the time goes in v3:
time: 424 us; the launch traced here: 423 us
  waiting for transfers between devices  328 us (77%)
  matrix products  43.2 us (10%)
  between operations  15.9 us (4%)
  local copies, waits for them, and re-layouts  13.1 us (3%)
  blocking collectives  10.7 us (3%)
  other arithmetic  8.51 us (2%)
    all_gather x1, waiting for transfers between devices, on_device(): gathered_in = lax.all_gather(elite_project, 'child', axis=1, tiled=True)  168 us
    all_gather x1, waiting for transfers between devices, output_rows(): gathered = lax.all_gather(shuffled, 'child', axis=1, tiled=True)  113 us
    all_gather x1, waiting for transfers between devices, on_device(): every_context = lax.all_gather(context, 'tensor', axis=1, tiled=True)  38.9 us
    dot_general x1, matrix products, on_device(): jnp.einsum('rd,dgc->rgc', tokens, child_in, preferred_element_type=jnp.fl...  23.9 us
    dot_general x1, matrix products, on_device(): jnp.einsum('rgc,dgc->rd', every_context, child_out, preferred_element_typ...  15.2 us
    all_gather x1, blocking collectives, output_rows(): every_group = lax.all_gather(elite_output, 'tensor', axis=2, tiled=True)  10.7 us
  transfers between devices with their start and end apart: 4, of which 4 were waited for; matrix products, arithmetic and copies ran while one was open for 11% of the time, Pallas kernels for 0%

profile of v3, /device:TPU:1, one launch (start us, length us, event | category | flops | bytes accessed | tf_op | source)
XLA Modules:
  0.0 423.1 jit_solution(16540738858953312930)
XLA Ops:
  6.5 0.7 all-gather.4.cloned.1.call-update
  7.3 10.7 %all_gather.14 = bf16[2,80,4,640]{3,1,0,2:T(8,128)(2,1)S(1)} all-gather(bf16[2,80,1,640]{3,1,0,2:T(8,128)(2,1)} %bitcast.75), channel_id=1, replica_groups=mesh['child'=64,'tensor'=4] {'tensor'}, dimensions={2}, use_global_device_ids=true | all-gather | bytes 1024000 | tf_op jit(solution)/shard_map/all_gather | solution.py:80
  18.1 3.2 collective-permute-start
  21.4 7.8 %collective-permute-done = bf16[2,20,4,640]{3,1,0,2:T(8,128)(2,1)S(1)} collective-permute-done((bf16[2,20,4,640]{3,1,0,2:T(8,128)(2,1)S(1)}, bf16[2,20,4,640]{3,1,0,2:T(8,128)(2,1)S(1)}, u32[]{:S(2)}, u32[]{:S(2)}) %collective-permute-start) | collective-permute-done | bytes 204832 | tf_op jit(solution)/shard_map/ppermute | solution.py:93
  29.2 0.8 copy.34
  30.1 1.2 dynamic_slice.18
  33.9 0.7 add_reduce_fusion
  34.7 0.9 convert_reduce_fusion
  35.6 1.0 fusion.26
  36.6 1.8 multiply_cosine_fusion
  38.4 167.9 %all-gather.4.cloned.1.call-done = bf16[2,5120,1,896]{3,1,2,0:T(8,128)(2,1)} async-done(((bf16[2,80,1,896]{3,1,2,0:T(8,128)(2,1)}), bf16[2,5120,1,896]{3,1,2,0:T(8,128)(2,1)}) %all-gather.4.cloned.1.call-update) | async-done | bytes 18350096 | tf_op jit(solution)/shard_map/all_gather | solution.py:123
  206.3 23.9 %add_bitcast_fusion = f32[512,1,896]{0,2,1:T(8,128)S(1)} fusion(bf16[512,5120]{1,0:T(8,128)(2,1)} %param.7, s32[]{:T(128)} %bitcast.2, s32[5120]{0:T(1024)S(1)} %add_multiply_fusion, bf16[2,5120,1,896]{3,1,2,0:T(8,128)(2,1)} %all-gather.4.cloned.1.call-done, s32[]{:T(128)S(6)} %select_n.19, f32[896]{0:T(1024)S(1)} %add_reduce_fusion), kind=kOutput, calls=%fused_computation.27 | convolution fusion | flops 4812767232 | bytes 16277508 | tf_op jit(solution)/shard_map/rd,dgc->rgc/dot_general | solution.py:145
  230.4 1.0 copy-done
  231.8 0.4 copy.40
  232.2 1.5 fusion.46
  233.8 1.4 fusion.27
  235.2 1.4 fusion.11
  236.6 1.1 fusion.10
  237.7 2.6 fusion.23
  240.4 1.1 copy.32
  241.5 113.1 %all-gather.8.cloned.1.call-done = bf16[2,1280,4,640]{3,2,0,1:T(4,128)(2,1)} async-done(((bf16[2,20,4,640]{3,2,0,1:T(4,128)(2,1)}), bf16[2,1280,4,640]{3,2,0,1:T(4,128)(2,1)}) %all-gather.8.cloned.1.call-update) | async-done | bytes 13107216 | tf_op jit(solution)/shard_map/all_gather | solution.py:95
  354.6 7.9 %constant_dynamic-slice_fusion = bf16[1,1280,4,640]{3,2,0,1:T(4,128)(2,1)} fusion(bf16[2,1280,4,640]{3,2,0,1:T(4,128)(2,1)} %all-gather.8.cloned.1.call-done, s32[]{:T(128)S(6)} %select_n.19), kind=kLoop, calls=%fused_computation.69 | loop fusion | bytes 13107204 | tf_op jit(solution)/shard_map/jit(dynamic_index_in_dim)/dynamic_slice | solution.py:97
  362.4 38.9 %all-gather.6.cloned.1.call-done = bf16[512,4,640]{2,0,1:T(8,128)(2,1)} async-done(((bf16[512,1,640]{2,0,1:T(8,128)(2,1)}), bf16[512,4,640]{2,0,1:T(8,128)(2,1)}) %all-gather.6.cloned.1.call-update) | async-done | bytes 2621456 | tf_op jit(solution)/shard_map/all_gather | solution.py:168
  401.3 15.2 %fusion.15 = bf16[512,1280]{1,0:T(8,128)(2,1)} fusion(bf16[512,4,640]{2,0,1:T(8,128)(2,1)} %all-gather.6.cloned.1.call-done, bf16[1,1280,4,640]{3,2,0,1:T(4,128)(2,1)} %constant_dynamic-slice_fusion, s32[]{:T(128)} %bitcast.2, s32[1280,4]{0,1:T(4,128)S(1)} %multiply_add_fusion), kind=kOutput, calls=%fused_computation.23 | convolution fusion | flops 3438018560 | bytes 10506244 | tf_op jit(solution)/shard_map/rgc,dgc->rd/dot_general | solution.py:169
  (15 shorter events, 0.8 us)
Async XLA Ops:
  6.5 199.7 %all-gather.4.cloned.1.call-start = ((), (), s32[]{:S(2)}) async-start(), calls=%async_computation | async-start | bytes 18636800 | tf_op jit(solution)/shard_map/all_gather | solution.py:123
  7.3 347.3 %all-gather.8.cloned.1.call-start = ((), (), s32[]{:S(2)}) async-start(), calls=%async_computation.2 | async-start | bytes 13312000 | tf_op jit(solution)/shard_map/all_gather | solution.py:95
  18.1 11.1 %collective-permute-start = (bf16[2,20,4,640]{3,1,0,2:T(8,128)(2,1)S(1)}, bf16[2,20,4,640]{3,1,0,2:T(8,128)(2,1)S(1)}, u32[]{:S(2)}, u32[]{:S(2)}) collective-permute-start(bf16[2,20,4,640]{3,1,0,2:T(8,128)(2,1)S(1)} %constant_dynamic-slice_fusion.1), channel_id=1, source_target_pairs={{0,0},{1,4},{2,8},{3,12},{4,16},{5,20},{6,24},{7,28},{8,32},{9,36}... | collective-permute-start | bytes 614408 | tf_op jit(solution)/shard_map/ppermute | solution.py:93
  30.0 371.3 %all-gather.6.cloned.1.call-start = ((), (), s32[]{:S(2)}) async-start(), calls=%async_computation.1 | async-start | bytes 3276800 | tf_op jit(solution)/shard_map/all_gather | solution.py:168
  230.2 1.3 copy-start
Sparse Core Ops, SparseCore 0:
  10.7 195.5 all-gather.3
  209.6 144.9 all-gather.7
  356.4 44.9 all-gather.5

commit v4 on v3

--- a/solution.py
+++ b/solution.py
@@ -75,7 +75,22 @@
     return (allowed, jnp.cos(angles), jnp.sin(angles))
 
 
-def output_rows(elite_output, parent_index, child_count, tensor_count, gather_rows):
+CHILD = ("cx", "cz", "cy")
+
+
+def ring_gather(block, axis_name, size):
+    forward = [(j, (j + 1) % size) for j in range(size)]
+    backward = [(j, (j - 1) % size) for j in range(size)]
+    from_prev = lax.ppermute(block, axis_name, forward)
+    from_next = lax.ppermute(block, axis_name, backward)
+    half = block.shape[0] // 2
+    far_low = lax.ppermute(from_prev[:half], axis_name, forward)
+    far_high = lax.ppermute(from_next[half:], axis_name, backward)
+    far = jnp.concatenate([far_low, far_high], axis=0)
+    return jnp.stack([block, from_next, far, from_prev])
+
+
+def shuffle_output_rows(elite_output, child_count, tensor_count):
     local_rows = elite_output.shape[1]
     every_group = lax.all_gather(elite_output, "tensor", axis=2, tiled=True)
     span = child_count // tensor_count
@@ -90,24 +105,17 @@
             )
     tensor_rank = lax.axis_index("tensor")
     mine = lax.dynamic_slice_in_dim(every_group, tensor_rank * piece, piece, axis=1)
-    shuffled = lax.ppermute(mine, ("child", "tensor"), pairs)
-    if gather_rows:
-        gathered = lax.all_gather(shuffled, "child", axis=1, tiled=True)
-        parent = parent_index[lax.axis_index("child")]
-        return lax.dynamic_index_in_dim(gathered, parent, 0, keepdims=False)
-    chosen = jnp.take(shuffled, parent_index, axis=0)
-    return lax.all_to_all(chosen, "child", split_axis=0, concat_axis=1, tiled=True)[0]
-
-
-GATHER_OUTPUT_ROWS = True
+    return lax.ppermute(mine, CHILD + ("tensor",), pairs)
 
 
 def on_device(
     tokens, episode, parent_index, mutation_seed, elite_project, elite_output, elite_bias
 ):
-    child_rank = lax.axis_index("child")
+    side = lax.axis_size("cx")
+    cx, cz, cy = (lax.axis_index(name) for name in CHILD)
+    child_rank = lax.axis_index(CHILD)
     tensor_rank = lax.axis_index("tensor")
-    child_count = lax.axis_size("child")
+    child_count = lax.axis_size(CHILD)
     tensor_count = lax.axis_size("tensor")
     kv_local = elite_project.shape[2]
     width_in = elite_project.shape[3]
@@ -120,18 +128,32 @@
     bias_base = out_base + D * KV_HEADS * width_out
     own_seed = mutation_seed[0]
     parent = parent_index[child_rank]
-    gathered_in = lax.all_gather(elite_project, "child", axis=1, tiled=True)
+    gathered_in = lax.all_gather(elite_project, CHILD, axis=1, tiled=True)
     arrived_in = lax.dynamic_index_in_dim(gathered_in, parent, 0, keepdims=False)
-    arrived_out = output_rows(
-        elite_output, parent_index, child_count, tensor_count, GATHER_OUTPUT_ROWS
-    )
+
+    shuffled = shuffle_output_rows(elite_output, child_count, tensor_count)
+    stage = ring_gather(shuffled, "cz", side)
+    stage = ring_gather(stage, "cx", side)
+    stage = ring_gather(stage, "cy", side)
+    picked = lax.dynamic_index_in_dim(stage, parent, 3, keepdims=False)
+    piece = picked.shape[3]
+    arrived_out = picked.reshape(child_count * piece, KV_HEADS, width_out)
+    offsets = jnp.arange(side, dtype=jnp.int32)
+    source_child = (
+        ((cx + offsets[None, :, None]) % side) * (side * side)
+        + ((cz + offsets[None, None, :]) % side) * side
+        + (cy + offsets[:, None, None]) % side
+    ).reshape(child_count)
+    out_rows = child_count * piece
+    own_rows = tensor_rank * out_rows + (
+        source_child[:, None] * piece + jnp.arange(piece, dtype=jnp.int32)[None, :]
+    ).reshape(out_rows)
+
     every_row = jnp.arange(D, dtype=jnp.int32)
     child_in = (
         arrived_in.astype(jnp.float32)
         + scale_in * gaussian(own_seed, counter_grid(every_row, group_ids, width_in, 0))
     ).astype(jnp.bfloat16)
-    out_rows = arrived_out.shape[0]
-    own_rows = tensor_rank * out_rows + jnp.arange(out_rows, dtype=jnp.int32)
     all_groups = jnp.arange(KV_HEADS, dtype=jnp.int32)
     child_out = (
         arrived_out.astype(jnp.float32)
@@ -164,25 +186,37 @@
     context = jnp.einsum(
         "gqrs,sgh->rgqh", probability, values, preferred_element_type=jnp.float32
     ).astype(jnp.bfloat16)
-    context = context.reshape(count_rows, kv_local, width_out)
-    every_context = lax.all_gather(context, "tensor", axis=1, tiled=True)
-    attended = jnp.einsum(
-        "rgc,dgc->rd", every_context, child_out, preferred_element_type=jnp.float32
-    )
-    return attended.astype(jnp.bfloat16)
+    context = context.reshape(count_rows, width_out)
+    around = ring_gather(context, "tensor", tensor_count)
+    every_context = jnp.take(around, (all_groups - tensor_rank) % tensor_count, axis=0)
+    shuffled_attended = jnp.einsum(
+        "grc,dgc->rd", every_context, child_out, preferred_element_type=jnp.float32
+    ).astype(jnp.bfloat16)
+    cxs = jnp.arange(child_count, dtype=jnp.int32) // (side * side)
+    czs = (jnp.arange(child_count, dtype=jnp.int32) // side) % side
+    cys = jnp.arange(child_count, dtype=jnp.int32) % side
+    block_of = (
+        ((cys - cy) % side) * (side * side) + ((cxs - cx) % side) * side + (czs - cz) % side
+    )
+    blocks = shuffled_attended.reshape(count_rows, child_count, piece)
+    return jnp.take(blocks, block_of, axis=1).reshape(count_rows, out_rows)
 
 
 def solution(mesh):
+    side = round(mesh.shape["child"] ** (1.0 / 3.0))
+    fine = jax.sharding.Mesh(
+        mesh.devices.reshape(side, side, side, mesh.shape["tensor"]), CHILD + ("tensor",)
+    )
     in_specs = (
-        P("child", None),
-        P("child", None),
+        P(CHILD, None),
+        P(CHILD, None),
         P(),
-        P("child"),
-        P(None, "child", "tensor", None),
-        P(None, "child", "tensor", None),
+        P(CHILD),
+        P(None, CHILD, "tensor", None),
+        P(None, CHILD, "tensor", None),
         P(None, "tensor", None),
     )
-    out_specs = P("child", "tensor")
+    out_specs = P(CHILD, "tensor")
     return jax.shard_map(
-        on_device, mesh=mesh, in_specs=in_specs, out_specs=out_specs, check_vma=False
-    )
+        on_device, mesh=fine, in_specs=in_specs, out_specs=out_specs, check_vma=False
+    )

time: 424 us -> 361 us (0.85); the launches traced: 423 us -> 355 us
  waiting for transfers between devices: 328 us -> 155 us
  starting transfers between devices: 3.33 us -> 68.4 us
  local copies, waits for them, and re-layouts: 13.1 us -> 39.4 us
  other arithmetic: 8.51 us -> 18 us
    all_gather x3 -> x1, waiting for transfers between devices: 320 us -> 0.01 us  [on_device(): gathered_in = lax.all_gather(elite_project, CHILD, axis=1, tiled=True)]
    ppermute x1 -> x17, waiting for transfers between devices: 7.82 us -> 155 us  [the longest x4 129 us: ring_gather(): from_next = lax.ppermute(block, axis_name, backward)]
    ppermute x1 -> x17, starting transfers between devices: 3.25 us -> 68.4 us  [the longest x4 39 us: ring_gather(): from_next = lax.ppermute(block, axis_name, backward)]
    dynamic_slice x2 -> x1, local copies, waits for them, and re-layouts: 7.94 us -> 0.07 us  [shuffle_output_rows(): lax.dynamic_slice_in_dim(every_group, tensor_rank * piece, piece, axis=1)]
    convert_element_type x0 -> x2, local copies, waits for them, and re-layouts: none -> 7.79 us  [the longest x1 7.14 us: on_device(): arrived_out.astype(jnp.float32)]
    ppermute x1 -> x6, local copies, waits for them, and re-layouts: 0.77 us -> 7.01 us  [the longest x2 2.75 us: ring_gather(): from_prev = lax.ppermute(block, axis_name, forward)]
    slice x0 -> x8, local copies, waits for them, and re-layouts: none -> 5.33 us  [the longest x4 3.35 us: ring_gather(): far_low = lax.ppermute(from_prev[:half], axis_name, forward)]
    another operation x0 -> x7, other arithmetic: none -> 5.08 us  [ring_gather(): return jnp.stack([block, from_next, far, from_prev])]
  transfers between devices with their start and end apart: 4 -> 18, of which waited for: 4 -> 9; matrix products, arithmetic and copies ran while one was open for 11% -> 22% of each run, Pallas kernels for 0% -> 0%
where the time goes in v4:
time: 361 us; the launch traced here: 355 us
  waiting for transfers between devices  155 us (43%)
  starting transfers between devices  68.4 us (19%)
  matrix products  46.2 us (13%)
  local copies, waits for them, and re-layouts  39.4 us (11%)
  other arithmetic  18 us (5%)
  between operations  16.6 us (5%)
  blocking collectives  10.7 us (3%)
    ppermute x4, waiting for transfers between devices, ring_gather(): from_next = lax.ppermute(block, axis_name, backward)  129 us
    ppermute x4, starting transfers between devices, ring_gather(): from_next = lax.ppermute(block, axis_name, backward)  39 us
    dot_general x1, matrix products, on_device(): jnp.einsum('rd,dgc->rgc', tokens, child_in, preferred_element_type=jnp.fl...  24.1 us
    ppermute x4, starting transfers between devices, ring_gather(): from_prev = lax.ppermute(block, axis_name, forward)  18 us
    dot_general x1, matrix products, on_device(): jnp.einsum('grc,dgc->rd', every_context, child_out, preferred_element_typ...  16.2 us
    ppermute x4, waiting for transfers between devices, ring_gather(): far_high = lax.ppermute(from_next[half:], axis_name, backward)  14.3 us
    all_gather x1, blocking collectives, shuffle_output_rows(): every_group = lax.all_gather(elite_output, 'tensor', axis=2, tiled=True)  10.7 us
    ppermute x1, waiting for transfers between devices, shuffle_output_rows(): return lax.ppermute(mine, CHILD + ('tensor',), pairs)  7.84 us
  transfers between devices with their start and end apart: 18, of which 9 were waited for; matrix products, arithmetic and copies ran while one was open for 22% of the time, Pallas kernels for 0%

profile of v4, /device:TPU:1, one launch (start us, length us, event | category | flops | bytes accessed | tf_op | source)
XLA Modules:
  0.0 354.7 jit_solution(12669793996958586175)
XLA Ops:
  7.3 10.7 %all_gather.7 = bf16[2,80,4,640]{3,1,0,2:T(8,128)(2,1)S(1)} all-gather(bf16[2,80,1,640]{3,1,0,2:T(8,128)(2,1)} %bitcast.117), channel_id=1, replica_groups=mesh['cx'=4,'cz'=4,'cy'=4,'tensor'=4] {'tensor'}, dimensions={2}, use_global_device_ids=true | all-gather | bytes 1024000 | tf_op jit(solution)/shard_map/all_gather | solution.py:95
  18.1 3.2 collective-permute-start.4
  21.3 7.8 %collective-permute-done.4 = bf16[2,20,4,640]{3,1,0,2:T(8,128)(2,1)S(1)} collective-permute-done((bf16[2,20,4,640]{3,1,0,2:T(8,128)(2,1)S(1)}, bf16[2,20,4,640]{3,1,0,2:T(8,128)(2,1)S(1)}, u32[]{:S(2)}, u32[]{:S(2)}) %collective-permute-start.4) | collective-permute-done | bytes 204832 | tf_op jit(solution)/shard_map/ppermute | solution.py:108
  29.2 23.3 %collective-permute-start.5 = (bf16[2,20,4,640]{3,1,0,2:T(8,128)(2,1)S(1)}, bf16[2,20,4,640]{3,1,0,2:T(8,128)(2,1)S(1)}, u32[]{:S(2)}, u32[]{:S(2)}) collective-permute-start(bf16[2,20,4,640]{3,1,0,2:T(8,128)(2,1)S(1)} %collective-permute-done.4), channel_id=1, source_target_pairs={{0,48},{16,0},{32,16},{48,32},{1,49},{17,1},{33,17},{49,33},{2,50}... | collective-permute-start | bytes 614408 | tf_op jit(solution)/shard_map/ppermute | solution.py:85
  53.5 9.8 %collective-permute-done.5 = bf16[2,20,4,640]{3,1,0,2:T(8,128)(2,1)S(1)} collective-permute-done((bf16[2,20,4,640]{3,1,0,2:T(8,128)(2,1)S(1)}, bf16[2,20,4,640]{3,1,0,2:T(8,128)(2,1)S(1)}, u32[]{:S(2)}, u32[]{:S(2)}) %collective-permute-start.5) | collective-permute-done | bytes 204832 | tf_op jit(solution)/shard_map/ppermute | solution.py:85
  63.9 4.0 %collective-permute-start.7 = (bf16[1,20,4,640]{3,1,0,2:T(8,128)(2,1)S(1)}, bf16[1,20,4,640]{3,1,0,2:T(8,128)(2,1)S(1)}, u32[]{:S(2)}, u32[]{:S(2)}) collective-permute-start(bf16[1,20,4,640]{3,1,0,2:T(8,128)(2,1)S(1)} %slice.72), channel_id=1, source_target_pairs={{0,16},{16,32},{32,48},{48,0},{1,17},{17,33},{33,49},{49,1},{2,18}... | collective-permute-start | bytes 307208 | tf_op jit(solution)/shard_map/ppermute | solution.py:87
  68.0 3.7 %collective-permute-done.8 = bf16[1,20,4,640]{3,1,0,2:T(8,128)(2,1)S(1)} collective-permute-done((bf16[1,20,4,640]{3,1,0,2:T(8,128)(2,1)S(1)}, bf16[1,20,4,640]{3,1,0,2:T(8,128)(2,1)S(1)}, u32[]{:S(2)}, u32[]{:S(2)}) %collective-permute-start.8) | collective-permute-done | bytes 102432 | tf_op jit(solution)/shard_map/ppermute | solution.py:88
  72.3 6.3 %collective-permute-start.9 = (bf16[4,2,20,4,640]{4,3,2,1,0:T(4,128)(2,1)S(1)}, bf16[4,2,20,4,640]{4,3,2,1,0:T(4,128)(2,1)S(1)}, u32[]{:S(2)}, u32[]{:S(2)}) collective-permute-start(bf16[4,2,20,4,640]{4,3,2,1,0:T(4,128)(2,1)S(1)} %copy.66), channel_id=1, source_target_pairs={{0,192},{64,0},{128,64},{192,128},{1,193},{65,1},{129,65},{193,129... | collective-permute-start | bytes 2457608 | tf_op jit(solution)/shard_map/ppermute | solution.py:85
  80.0 30.2 %collective-permute-done.9 = bf16[4,2,20,4,640]{4,3,2,1,0:T(4,128)(2,1)S(1)} collective-permute-done((bf16[4,2,20,4,640]{4,3,2,1,0:T(4,128)(2,1)S(1)}, bf16[4,2,20,4,640]{4,3,2,1,0:T(4,128)(2,1)S(1)}, u32[]{:S(2)}, u32[]{:S(2)}) %collective-permute-start.9) | collective-permute-done | bytes 819232 | tf_op jit(solution)/shard_map/ppermute | solution.py:85
  112.4 10.6 %collective-permute-done.12 = bf16[2,2,20,4,640]{4,2,1,3,0:T(8,128)(2,1)S(1)} collective-permute-done((bf16[2,2,20,4,640]{4,2,1,3,0:T(8,128)(2,1)S(1)}, bf16[2,2,20,4,640]{4,2,1,3,0:T(8,128)(2,1)S(1)}, u32[]{:S(2)}, u32[]{:S(2)}) %collective-permute-start.12) | collective-permute-done | bytes 409632 | tf_op jit(solution)/shard_map/ppermute | solution.py:88
  127.4 2.9 copy.72
  130.3 8.3 %collective-permute-start.13 = (bf16[4,4,2,20,4,640]{5,4,3,2,1,0:T(4,128)(2,1)}, bf16[4,4,2,20,4,640]{5,4,3,2,1,0:T(4,128)(2,1)S(1)}, u32[]{:S(2)}, u32[]{:S(2)}) collective-permute-start(bf16[4,4,2,20,4,640]{5,4,3,2,1,0:T(4,128)(2,1)} %copy.72), channel_id=1, source_target_pairs={{0,12},{4,0},{8,4},{12,8},{1,13},{5,1},{9,5},{13,9},{2,14},{6,2},{... | collective-permute-start | bytes 9830408 | tf_op jit(solution)/shard_map/ppermute | solution.py:85
  138.6 11.1 %collective-permute-start.14 = (bf16[4,4,2,20,4,640]{5,4,3,2,1,0:T(4,128)(2,1)}, bf16[4,4,2,20,4,640]{5,4,3,2,1,0:T(4,128)(2,1)}, u32[]{:S(2)}, u32[]{:S(2)}) collective-permute-start(bf16[4,4,2,20,4,640]{5,4,3,2,1,0:T(4,128)(2,1)} %copy.72), channel_id=1, source_target_pairs={{0,4},{4,8},{8,12},{12,0},{1,5},{5,9},{9,13},{13,1},{2,6},{6,10},{... | collective-permute-start | bytes 9830408 | tf_op jit(solution)/shard_map/ppermute | solution.py:84
  159.5 79.8 %collective-permute-done.13 = bf16[4,4,2,20,4,640]{5,4,3,2,1,0:T(4,128)(2,1)S(1)} collective-permute-done((bf16[4,4,2,20,4,640]{5,4,3,2,1,0:T(4,128)(2,1)}, bf16[4,4,2,20,4,640]{5,4,3,2,1,0:T(4,128)(2,1)S(1)}, u32[]{:S(2)}, u32[]{:S(2)}) %collective-permute-start.13) | collective-permute-done | bytes 3276832 | tf_op jit(solution)/shard_map/ppermute | solution.py:85
  243.0 3.2 slice.76
  246.2 24.1 %add_bitcast_fusion = f32[512,1,896]{0,2,1:T(8,128)S(1)} fusion(bf16[512,5120]{1,0:T(8,128)(2,1)} %param.7, s32[]{:T(128)} %bitcast.2, s32[5120]{0:T(1024)} %add_multiply_fusion.1, bf16[2,5120,1,896]{3,1,2,0:T(8,128)(2,1)} %all-gather.2.cloned.1.call-done, s32[]{:T(128)S(6)} %select_n.226, f32[896]{0:T(1024)S(1)} %copy-done.7), kind=kOutput, calls=%fused_computation.43 | convolution fusion | flops 4812767232 | bytes 16277508 | tf_op jit(solution)/shard_map/rd,dgc->rgc/dot_general | solution.py:167
  273.5 2.6 copy.86
  276.0 2.6 copy.85
  284.2 3.5 fusion.29
  289.9 4.4 %collective-permute-start.1 = (bf16[512,640]{1,0:T(8,128)(2,1)}, bf16[512,640]{1,0:T(8,128)(2,1)S(1)}, u32[]{:S(2)}, u32[]{:S(2)}) collective-permute-start(bf16[512,640]{1,0:T(8,128)(2,1)} %copy.62), channel_id=1, source_target_pairs={{0,1},{1,2},{2,3},{3,0},{4,5},{5,6},{6,7},{7,4},{8,9},{9,10},{10,1... | collective-permute-start | bytes 1966088 | tf_op jit(solution)/shard_map/ppermute | solution.py:84
  296.1 2.6 copy.101
  302.8 9.0 %collective-permute-done = bf16[512,640]{1,0:T(8,128)(2,1)S(1)} collective-permute-done((bf16[512,640]{1,0:T(8,128)(2,1)}, bf16[512,640]{1,0:T(8,128)(2,1)S(1)}, u32[]{:S(2)}, u32[]{:S(2)}) %collective-permute-start) | collective-permute-done | bytes 655392 | tf_op jit(solution)/shard_map/ppermute | solution.py:85
  316.0 7.1 %copy.78 = f32[4,4,4,1,20,4,640]{6,5,4,2,1,0,3:T(4,128)} copy(f32[4,4,4,1,20,4,640]{6,4,3,5,2,1,0:T(8,128)S(1)} %fusion.11) | data formatting | bytes 26214400 | tf_op jit(solution)/shard_map/convert_element_type | solution.py:159
  327.7 16.2 %fusion.19 = bf16[512,1280]{1,0:T(8,128)(2,1)S(1)} fusion(f32[1280,4,640]{2,1,0:T(4,128)} %bitcast.106, s32[]{:T(128)} %bitcast.2, s32[1280,4]{0,1:T(4,128)S(1)} %multiply_add_fusion, bf16[4,512,640]{2,1,0:T(8,128)(2,1)} %gather_fusion, pred[4]{0:T(512)(128)(4,1)S(1)} %copy-done.11), kind=kOutput, calls=%fused_computation.36 | convolution fusion | flops 3436052480 | bytes 17059848 | tf_op jit(solution)/shard_map/grc,dgc->rd/dot_general | solution.py:192
  (110 shorter events, 50.9 us)
Async XLA Ops:
  6.5 239.7 %all-gather.2.cloned.1.call-start = ((), (), s32[]{:S(2)}) async-start(), calls=%async_computation | async-start | bytes 18636800 | tf_op jit(solution)/shard_map/all_gather | solution.py:131
  18.1 11.1 %collective-permute-start.4 = (bf16[2,20,4,640]{3,1,0,2:T(8,128)(2,1)S(1)}, bf16[2,20,4,640]{3,1,0,2:T(8,128)(2,1)S(1)}, u32[]{:S(2)}, u32[]{:S(2)}) collective-permute-start(bf16[2,20,4,640]{3,1,0,2:T(8,128)(2,1)S(1)} %constant_dynamic-slice_fusion), channel_id=1, source_target_pairs={{0,0},{1,4},{2,8},{3,12},{4,16},{5,20},{6,24},{7,28},{8,32},{9,36}... | collective-permute-start | bytes 614408 | tf_op jit(solution)/shard_map/ppermute | solution.py:108
  29.2 34.1 %collective-permute-start.5 = (bf16[2,20,4,640]{3,1,0,2:T(8,128)(2,1)S(1)}, bf16[2,20,4,640]{3,1,0,2:T(8,128)(2,1)S(1)}, u32[]{:S(2)}, u32[]{:S(2)}) collective-permute-start(bf16[2,20,4,640]{3,1,0,2:T(8,128)(2,1)S(1)} %collective-permute-done.4), channel_id=1, source_target_pairs={{0,48},{16,0},{32,16},{48,32},{1,49},{17,1},{33,17},{49,33},{2,50}... | collective-permute-start | bytes 614408 | tf_op jit(solution)/shard_map/ppermute | solution.py:85
  52.5 11.4 %collective-permute-start.6 = (bf16[2,20,4,640]{3,1,0,2:T(8,128)(2,1)S(1)}, bf16[2,20,4,640]{3,1,0,2:T(8,128)(2,1)S(1)}, u32[]{:S(2)}, u32[]{:S(2)}) collective-permute-start(bf16[2,20,4,640]{3,1,0,2:T(8,128)(2,1)S(1)} %collective-permute-done.4), channel_id=1, source_target_pairs={{0,16},{16,32},{32,48},{48,0},{1,17},{17,33},{33,49},{49,1},{2,18}... | collective-permute-start | bytes 614408 | tf_op jit(solution)/shard_map/ppermute | solution.py:84
  63.3 8.4 %collective-permute-start.8 = (bf16[1,20,4,640]{3,1,0,2:T(8,128)(2,1)S(1)}, bf16[1,20,4,640]{3,1,0,2:T(8,128)(2,1)S(1)}, u32[]{:S(2)}, u32[]{:S(2)}) collective-permute-start(bf16[1,20,4,640]{3,1,0,2:T(8,128)(2,1)S(1)} %slice.73), channel_id=1, source_target_pairs={{0,48},{16,0},{32,16},{48,32},{1,49},{17,1},{33,17},{49,33},{2,50}... | collective-permute-start | bytes 307208 | tf_op jit(solution)/shard_map/ppermute | solution.py:88
  63.9 7.8 %collective-permute-start.7 = (bf16[1,20,4,640]{3,1,0,2:T(8,128)(2,1)S(1)}, bf16[1,20,4,640]{3,1,0,2:T(8,128)(2,1)S(1)}, u32[]{:S(2)}, u32[]{:S(2)}) collective-permute-start(bf16[1,20,4,640]{3,1,0,2:T(8,128)(2,1)S(1)} %slice.72), channel_id=1, source_target_pairs={{0,16},{16,32},{32,48},{48,0},{1,17},{17,33},{33,49},{49,1},{2,18}... | collective-permute-start | bytes 307208 | tf_op jit(solution)/shard_map/ppermute | solution.py:87
  72.3 37.8 %collective-permute-start.9 = (bf16[4,2,20,4,640]{4,3,2,1,0:T(4,128)(2,1)S(1)}, bf16[4,2,20,4,640]{4,3,2,1,0:T(4,128)(2,1)S(1)}, u32[]{:S(2)}, u32[]{:S(2)}) collective-permute-start(bf16[4,2,20,4,640]{4,3,2,1,0:T(4,128)(2,1)S(1)} %copy.66), channel_id=1, source_target_pairs={{0,192},{64,0},{128,64},{192,128},{1,193},{65,1},{129,65},{193,129... | collective-permute-start | bytes 2457608 | tf_op jit(solution)/shard_map/ppermute | solution.py:85
  78.5 32.7 %collective-permute-start.10 = (bf16[4,2,20,4,640]{4,3,2,1,0:T(4,128)(2,1)S(1)}, bf16[4,2,20,4,640]{4,3,2,1,0:T(4,128)(2,1)S(1)}, u32[]{:S(2)}, u32[]{:S(2)}) collective-permute-start(bf16[4,2,20,4,640]{4,3,2,1,0:T(4,128)(2,1)S(1)} %copy.66), channel_id=1, source_target_pairs={{0,64},{64,128},{128,192},{192,0},{1,65},{65,129},{129,193},{193,1... | collective-permute-start | bytes 2457608 | tf_op jit(solution)/shard_map/ppermute | solution.py:84
  110.3 12.7 %collective-permute-start.12 = (bf16[2,2,20,4,640]{4,2,1,3,0:T(8,128)(2,1)S(1)}, bf16[2,2,20,4,640]{4,2,1,3,0:T(8,128)(2,1)S(1)}, u32[]{:S(2)}, u32[]{:S(2)}) collective-permute-start(bf16[2,2,20,4,640]{4,2,1,3,0:T(8,128)(2,1)S(1)} %copy.99), channel_id=1, source_target_pairs={{0,192},{64,0},{128,64},{192,128},{1,193},{65,1},{129,65},{193,129... | collective-permute-start | bytes 1228808 | tf_op jit(solution)/shard_map/ppermute | solution.py:88
  111.5 13.4 %collective-permute-start.11 = (bf16[2,2,20,4,640]{4,2,1,3,0:T(8,128)(2,1)S(1)}, bf16[2,2,20,4,640]{4,2,1,3,0:T(8,128)(2,1)S(1)}, u32[]{:S(2)}, u32[]{:S(2)}) collective-permute-start(bf16[2,2,20,4,640]{4,2,1,3,0:T(8,128)(2,1)S(1)} %copy.100), channel_id=1, source_target_pairs={{0,64},{64,128},{128,192},{192,0},{1,65},{65,129},{129,193},{193,1... | collective-permute-start | bytes 1228808 | tf_op jit(solution)/shard_map/ppermute | solution.py:87
  127.4 22.4 %copy-start.10 = (s32[64]{0:T(128)S(1)}, s32[64]{0:T(128)}, u32[]{:S(2)}) copy-start(s32[64]{0:T(128)} %param.9) | copy-start | bytes 772
  127.4 26.9 %copy-start.9 = (f32[2,1,896]{2,1,0:T(1,128)S(1)}, f32[2,1,896]{2,1,0:T(1,128)}, u32[]{:S(2)}) copy-start(f32[2,1,896]{2,1,0:T(1,128)} %param.13) | copy-start | bytes 21508
  127.4 29.9 %copy-start.5 = (s32[1,512]{1,0:T(1,128)S(1)}, s32[1,512]{1,0:T(1,128)}, u32[]{:S(2)}) copy-start(s32[1,512]{1,0:T(1,128)} %param.8) | copy-start | bytes 6148
  130.3 109.1 %collective-permute-start.13 = (bf16[4,4,2,20,4,640]{5,4,3,2,1,0:T(4,128)(2,1)}, bf16[4,4,2,20,4,640]{5,4,3,2,1,0:T(4,128)(2,1)S(1)}, u32[]{:S(2)}, u32[]{:S(2)}) collective-permute-start(bf16[4,4,2,20,4,640]{5,4,3,2,1,0:T(4,128)(2,1)} %copy.72), channel_id=1, source_target_pairs={{0,12},{4,0},{8,4},{12,8},{1,13},{5,1},{9,5},{13,9},{2,14},{6,2},{... | collective-permute-start | bytes 9830408 | tf_op jit(solution)/shard_map/ppermute | solution.py:85
  138.6 104.4 %collective-permute-start.14 = (bf16[4,4,2,20,4,640]{5,4,3,2,1,0:T(4,128)(2,1)}, bf16[4,4,2,20,4,640]{5,4,3,2,1,0:T(4,128)(2,1)}, u32[]{:S(2)}, u32[]{:S(2)}) collective-permute-start(bf16[4,4,2,20,4,640]{5,4,3,2,1,0:T(4,128)(2,1)} %copy.72), channel_id=1, source_target_pairs={{0,4},{4,8},{8,12},{12,0},{1,5},{5,9},{9,13},{13,1},{2,6},{6,10},{... | collective-permute-start | bytes 9830408 | tf_op jit(solution)/shard_map/ppermute | solution.py:84
  157.7 88.5 %copy-start.7 = (f32[896]{0:T(1024)S(1)}, f32[896]{0:T(1024)}, u32[]{:S(2)}) copy-start(f32[896]{0:T(1024)} %add_reduce_fusion) | copy-start | bytes 10756
  241.2 57.6 %collective-permute-start.16 = (bf16[2,4,2,20,4,640]{5,4,3,2,1,0:T(4,128)(2,1)}, bf16[2,4,2,20,4,640]{5,4,3,2,1,0:T(4,128)(2,1)}, u32[]{:S(2)}, u32[]{:S(2)}) collective-permute-start(bf16[2,4,2,20,4,640]{5,4,3,2,1,0:T(4,128)(2,1)} %slice.77), channel_id=1, source_target_pairs={{0,12},{4,0},{8,4},{12,8},{1,13},{5,1},{9,5},{13,9},{2,14},{6,2},{... | collective-permute-start | bytes 4915208 | tf_op jit(solution)/shard_map/ppermute | solution.py:88
  246.2 54.3 %collective-permute-start.15 = (bf16[2,4,2,20,4,640]{5,4,3,2,1,0:T(4,128)(2,1)}, bf16[2,4,2,20,4,640]{5,4,3,2,1,0:T(4,128)(2,1)}, u32[]{:S(2)}, u32[]{:S(2)}) collective-permute-start(bf16[2,4,2,20,4,640]{5,4,3,2,1,0:T(4,128)(2,1)} %slice.76), channel_id=1, source_target_pairs={{0,4},{4,8},{8,12},{12,0},{1,5},{5,9},{9,13},{13,1},{2,6},{6,10},{... | collective-permute-start | bytes 4915208 | tf_op jit(solution)/shard_map/ppermute | solution.py:87
  289.9 22.1 %collective-permute-start.1 = (bf16[512,640]{1,0:T(8,128)(2,1)}, bf16[512,640]{1,0:T(8,128)(2,1)S(1)}, u32[]{:S(2)}, u32[]{:S(2)}) collective-permute-start(bf16[512,640]{1,0:T(8,128)(2,1)} %copy.62), channel_id=1, source_target_pairs={{0,1},{1,2},{2,3},{3,0},{4,5},{5,6},{6,7},{7,4},{8,9},{9,10},{10,1... | collective-permute-start | bytes 1966088 | tf_op jit(solution)/shard_map/ppermute | solution.py:84
  294.3 17.6 %collective-permute-start = (bf16[512,640]{1,0:T(8,128)(2,1)}, bf16[512,640]{1,0:T(8,128)(2,1)S(1)}, u32[]{:S(2)}, u32[]{:S(2)}) collective-permute-start(bf16[512,640]{1,0:T(8,128)(2,1)} %copy.62), channel_id=1, source_target_pairs={{0,3},{1,0},{2,1},{3,2},{4,7},{5,4},{6,5},{7,6},{8,11},{9,8},{10,9... | collective-permute-start | bytes 1966088 | tf_op jit(solution)/shard_map/ppermute | solution.py:85
  302.2 11.6 %copy-start = (bf16[1,4,4,2,20,4,640]{6,4,3,5,2,1,0:T(8,128)(2,1)S(1)}, bf16[1,4,4,2,20,4,640]{6,4,3,5,2,1,0:T(8,128)(2,1)}, u32[]{:S(2)}) copy-start(bf16[1,4,4,2,20,4,640]{6,4,3,5,2,1,0:T(8,128)(2,1)} %get-tuple-element.6) | copy-start | bytes 9830404
  311.9 11.5 %collective-permute-start.3 = (bf16[256,640]{1,0:T(8,128)(2,1)S(1)}, bf16[256,640]{1,0:T(8,128)(2,1)S(1)}, u32[]{:S(2)}, u32[]{:S(2)}) collective-permute-start(bf16[256,640]{1,0:T(8,128)(2,1)S(1)} %slice.71), channel_id=1, source_target_pairs={{0,3},{1,0},{2,1},{3,2},{4,7},{5,4},{6,5},{7,6},{8,11},{9,8},{10,9... | collective-permute-start | bytes 983048 | tf_op jit(solution)/shard_map/ppermute | solution.py:88
  312.0 11.4 %collective-permute-start.2 = (bf16[256,640]{1,0:T(8,128)(2,1)S(1)}, bf16[256,640]{1,0:T(8,128)(2,1)S(1)}, u32[]{:S(2)}, u32[]{:S(2)}) collective-permute-start(bf16[256,640]{1,0:T(8,128)(2,1)S(1)} %slice.70), channel_id=1, source_target_pairs={{0,1},{1,2},{2,3},{3,0},{4,5},{5,6},{6,7},{7,4},{8,9},{9,10},{10,1... | collective-permute-start | bytes 983048 | tf_op jit(solution)/shard_map/ppermute | solution.py:87
  315.9 7.2 %copy-start.1 = (bf16[128,5,512]{2,0,1:T(8,128)(2,1)S(1)}, bf16[128,5,512]{2,0,1:T(8,128)(2,1)}, u32[]{:S(2)}) copy-start(bf16[128,5,512]{2,0,1:T(8,128)(2,1)} %fusion.29) | copy-start | bytes 1966084
  (6 other events, 19.3 us)
Sparse Core Ops, SparseCore 0:
  10.7 201.1 all-gather.1
